TPU v7x, 512 devices: a whole 4x4x16 slice. The times are simulated.
512 devices in a mesh: lon: 32 (over z, x_hi), lat: 16 (over x_lo, y, core).
Axes of the slice: x: 4 (x_hi: 2, x_lo: 2; x = x_hi * 2 + x_lo), y: 4, z: 16, core: 2. Of those that a mesh axis runs over, the one named last changes fastest.
Arguments:
- elevation: float32 [12, 1536, 4096], P(None, 'lat', 'lon'), may hold values from -6 to 6
- equilibrium: float32 [12, 1536, 4096], P(None, 'lat', 'lon'), may hold values from -4 to 4
- transport_u: float32 [12, 1536, 4096], P(None, 'lat', 'lon'), may hold values from -4 to 4
- transport_v: float32 [12, 1536, 4096], P(None, 'lat', 'lon'), may hold values from -4 to 4
- ocean_depth: float32 [1536, 4096], P('lat', 'lon'), may hold values from 0.3 to 3
- bottom_drag: float32 [1536, 4096], P('lat', 'lon'), may hold values from 0.2 to 2
- wet_mask: int32 [1536, 4096], P('lat', 'lon'), may hold values 0 or 1
- lon_green: float32 [4096, 128], P('lon'), may hold values from -0.5 to 0.5
- lat_green: float32 [1536, 49152], P('lat', 'lon'), may hold values from -0.0546875 to 0.0546875
Outputs:
- elevation_next: float32 [12, 1536, 4096], P(None, 'lat', 'lon')
- transport_u_next: float32 [12, 1536, 4096], P(None, 'lat', 'lon')
- transport_v_next: float32 [12, 1536, 4096], P(None, 'lat', 'lon')
All inputs are finite; a program needn't handle non-finite values. No bound on the sum of `wet_mask` on one device may be relied on, other than what follows from the above.
Results may differ from a plain program's by a relative error of at most 0.0001.
Values sent between devices are 32-bit elements; how exact they have to be, the bound alone decides.
No kernel may reach another device: no remote copies, remote signals or barrier semaphores. Data moves between devices by JAX's collectives and lax.ppermute only.
A program may use at most 64 MiB of HBM per device.

v0:
```python
import math
import jax
import jax.numpy as jnp
from jax import lax
from jax.sharding import Mesh
from jax.sharding import PartitionSpec as P

FREQS = [1.9323, 2.0, 1.896, 2.0055, 1.0027, 0.9295]
VISCOSITY = 0.5
HALO = 3
LAT = ("chip", "core")


def lat_index():
    return lax.axis_index("chip") * lax.axis_size("core") + lax.axis_index("core")


def lat_size():
    return lax.axis_size("chip") * lax.axis_size("core")


def widen_lon(array, width, dim):
    size, length = (lax.axis_size("lon"), array.shape[dim])
    up = [(i, (i + 1) % size) for i in range(size)]
    down = [(j, i) for i, j in up]
    last = lax.slice_in_dim(array, length - width, length, axis=dim)
    initial = lax.slice_in_dim(array, 0, width, axis=dim)
    before = lax.ppermute(last, "lon", up)
    after = lax.ppermute(initial, "lon", down)
    return jnp.concatenate([before, array, after], axis=dim)


def widen_lat(array, width, dim):
    size, length = (lat_size(), array.shape[dim])
    up = [(i, i + 1) for i in range(size - 1)]
    down = [(j, i) for i, j in up]
    last = lax.slice_in_dim(array, length - width, length, axis=dim)
    initial = lax.slice_in_dim(array, 0, width, axis=dim)
    before = lax.ppermute(last, LAT, up)
    after = lax.ppermute(initial, LAT, down)
    return jnp.concatenate([before, array, after], axis=dim)


def row_terms(rows, nlat):
    angle = (-80.0 + 160.0 * (rows.astype(jnp.float32) + 0.5) / nlat) * (math.pi / 180.0)
    return ((1.0 / jnp.cos(angle))[:, None], (2.0 * jnp.sin(angle))[:, None])


def slopes(potential_ext, stretch):
    east_slope = (potential_ext[:, 1:-1, 2:] - potential_ext[:, 1:-1, :-2]) * 0.5 * stretch
    north_slope = (potential_ext[:, 2:, 1:-1] - potential_ext[:, :-2, 1:-1]) * 0.5
    return (east_slope, north_slope)


def solve_cells(push_u, push_v, drag_field, wet_frac, coriolis):
    damping = drag_field + 4.0 * VISCOSITY
    frequency = jnp.array(FREQS, jnp.float32)[:, None, None]
    det_real = damping * damping - frequency * frequency + coriolis * coriolis
    det_imag = 2.0 * damping * frequency
    magnitude = det_real * det_real + det_imag * det_imag

    def combine(first, second, factor):
        top_real = damping * first[:6] - frequency * first[6:] + factor * coriolis * second[:6]
        top_imag = damping * first[6:] + frequency * first[:6] + factor * coriolis * second[6:]
        out_real = (top_real * det_real + top_imag * det_imag) / magnitude
        out_imag = (top_imag * det_real - top_real * det_imag) / magnitude
        return wet_frac * jnp.concatenate([out_real, out_imag], axis=0)

    return jnp.concatenate([combine(push_u, push_v, 1.0), combine(push_v, push_u, -1.0)], axis=0)


def inner(field, trim):
    return field[..., trim : field.shape[-2] - trim, trim : field.shape[-1] - trim]


def relax(flow_ext, east_slope, north_slope, depth_field, drag_field, wet_frac, coriolis):
    beside_all = (
        flow_ext[:, :-2, 1:-1]
        + flow_ext[:, 2:, 1:-1]
        + flow_ext[:, 1:-1, :-2]
        + flow_ext[:, 1:-1, 2:]
    )
    push_u = -depth_field * east_slope + VISCOSITY * beside_all[:12]
    push_v = -depth_field * north_slope + VISCOSITY * beside_all[12:]
    return solve_cells(push_u, push_v, drag_field, wet_frac, coriolis)


def surface(east_ext, north_ext, stretch, wet_frac):
    spread = (east_ext[:, :, 2:] - east_ext[:, :, :-2]) * 0.5 * stretch + (
        north_ext[:, 2:, :] - north_ext[:, :-2, :]
    ) * 0.5
    frequency = jnp.array(FREQS, jnp.float32)[:, None, None]
    return wet_frac * jnp.concatenate([-spread[6:] / frequency, spread[:6] / frequency], axis=0)


def per_device(
    elevation,
    equilibrium,
    transport_u,
    transport_v,
    ocean_depth,
    bottom_drag,
    wet_mask,
    lon_green,
    lat_green,
):
    rows_here = elevation.shape[1]
    total_rows = rows_here * lat_size()
    wet_frac = wet_mask.astype(jnp.float32)
    source = wet_frac * elevation
    mixed = jnp.einsum("krj,cj->krc", source, lon_green, precision=lax.Precision.HIGHEST)
    columns = mixed.shape[2]
    edge_rows = jnp.concatenate([lon_green[:HALO], lon_green[columns - HALO :]], axis=0)
    edges = jnp.einsum("ej,krj->ker", edge_rows, source, precision=lax.Precision.HIGHEST)
    spare = 8 * ((2 * HALO + 7) // 8)
    edges = jnp.pad(edges, ((0, 0), (0, spare - 2 * HALO), (0, columns - rows_here)))
    packed = jnp.concatenate([mixed, edges], axis=1)
    gathered = lax.all_gather(packed, LAT, axis=1, tiled=True)
    fields = jnp.stack([ocean_depth, bottom_drag, wet_frac], axis=0)
    stack = jnp.concatenate([elevation - equilibrium, transport_u, transport_v, fields], axis=0)
    stack = widen_lat(widen_lon(stack, HALO, 2), HALO, 1)
    green_ext = widen_lat(lat_green, HALO, 0)
    blocks = lat_size()
    block = rows_here + spare
    green_blocks = green_ext.reshape(green_ext.shape[0], blocks, rows_here)
    lanes = gathered.reshape(12, blocks, block, columns)[
        :, :, rows_here : rows_here + 2 * HALO, :rows_here
    ]
    edge_sal = jnp.einsum("rbj,kbej->kre", green_blocks, lanes, precision=lax.Precision.HIGHEST)
    size = lax.axis_size("lon")
    up = [(i, (i + 1) % size) for i in range(size)]
    down = [(j, i) for i, j in up]
    before = lax.ppermute(edge_sal[:, :, HALO:], "lon", up)
    after = lax.ppermute(edge_sal[:, :, :HALO], "lon", down)
    green_pad = jnp.pad(green_blocks, ((0, 0), (0, 0), (0, spare))).reshape(green_ext.shape[0], -1)
    sal = jnp.einsum("rs,ksc->krc", green_pad, gathered, precision=lax.Precision.HIGHEST)
    sal = jnp.concatenate([before, sal, after], axis=2)
    potential = stack[:12] - sal
    flows = stack[12:36]
    depth_ext, drag_ext, wet_ext = (stack[36], stack[37], stack[38])
    first_row = lat_index() * rows_here - HALO
    stretch, coriolis = row_terms(first_row + jnp.arange(rows_here + 2 * HALO), total_rows)
    east_slope, north_slope = slopes(potential, stretch[1:-1])
    flows = relax(
        flows,
        east_slope,
        north_slope,
        inner(depth_ext, 1),
        inner(drag_ext, 1),
        inner(wet_ext, 1),
        coriolis[1:-1],
    )
    flows = relax(
        flows,
        inner(east_slope, 1),
        inner(north_slope, 1),
        inner(depth_ext, 2),
        inner(drag_ext, 2),
        inner(wet_ext, 2),
        coriolis[2:-2],
    )
    east_ext = flows[:12, 1:-1, :]
    north_ext = flows[12:, :, 1:-1]
    elevation_next = surface(east_ext, north_ext, stretch[HALO:-HALO], wet_frac)
    flows = inner(flows, 1)
    return (elevation_next, flows[:12], flows[12:])


def solution(mesh):
    lat_devices = mesh.shape["lat"]
    cores = 2 if lat_devices % 2 == 0 else 1
    devices = mesh.devices.reshape(mesh.shape["lon"], lat_devices // cores, cores)
    split = Mesh(devices, ("lon", "chip", "core"))
    grid = P(None, LAT, "lon")
    plane = P(LAT, "lon")
    placed = (grid, grid, grid, grid, plane, plane, plane, P("lon", None), plane)
    return jax.shard_map(
        per_device, mesh=split, in_specs=placed, out_specs=(grid, grid, grid), check_vma=False
    )
```

profile of v0, /device:TPU:1, one launch (start us, length us, event | category | flops | bytes accessed | tf_op | source)
XLA Modules:
  0.0 135.8 jit_solution(12874723545811327905)
XLA Ops:
  8.8 1.7 %fusion.45 = f32[12,96,128]{2,1,0:T(8,128)S(1)} fusion(f32[12,96,128]{2,1,0:T(8,128)} %param.12, f32[96,128]{1,0:T(8,128)S(1)} %convert_element_type.10, f32[128,128]{1,0:T(8,128)} %param.19), kind=kOutput, calls=%fused_computation.99 | convolution fusion | flops 226639872 | bytes 1294336 | tf_op jit(solution)/shard_map/krj,cj->krc/dot_general | solution.py:111
  10.5 1.2 convolution_bitcast_fusion.2
  12.7 4.6 %collective-permute-start.4 = (f32[3,1536]{1,0:T(4,128)S(1)}, f32[3,1536]{1,0:T(4,128)S(1)}, u32[]{:S(2)}, u32[]{:S(2)}) collective-permute-start(f32[3,1536]{1,0:T(4,128)S(1)} %get-tuple-element.41), channel_id=1, source_target_pairs={{0,1},{1,2},{2,3},{3,4},{4,5},{5,6},{6,7},{7,8},{8,9},{9,10},{10,1... | collective-permute-start | bytes 55304 | tf_op jit(solution)/shard_map/ppermute | solution.py:39
  17.3 5.6 %collective-permute-start.5 = (f32[3,1536]{1,0:T(4,128)S(1)}, f32[3,1536]{1,0:T(4,128)S(1)}, u32[]{:S(2)}, u32[]{:S(2)}) collective-permute-start(f32[3,1536]{1,0:T(4,128)S(1)} %get-tuple-element.42), channel_id=1, source_target_pairs={{1,0},{2,1},{3,2},{4,3},{5,4},{6,5},{7,6},{8,7},{9,8},{10,9},{11,1... | collective-permute-start | bytes 55304 | tf_op jit(solution)/shard_map/ppermute | solution.py:40
  22.9 1.1 subtract_dynamic-update-slice_fusion
  24.1 1.1 constant_dynamic-update-slice_fusion.1
  25.4 2.6 %fusion.57 = (f32[39,96,3]{2,1,0:T(8,128)}, f32[39,96,3]{2,1,0:T(8,128)}) fusion(f32[39,96,128]{2,1,0:T(8,128)S(1)} %bitcast_dynamic-update-slice_fusion), kind=kLoop, calls=%fused_computation.140 | loop fusion | bytes 179712 | tf_op jit(solution)/shard_map/slice | solution.py:26
  28.0 2.1 %copy.21 = f32[39,96,3]{1,0,2:T(8,128)S(1)} copy(f32[39,96,3]{2,1,0:T(8,128)} %get-tuple-element.35) | data formatting | bytes 89856 | tf_op jit(solution)/shard_map/slice | solution.py:27
  30.1 10.0 %collective-permute-start.1 = (f32[39,96,3]{1,0,2:T(8,128)S(1)}, f32[39,96,3]{1,0,2:T(8,128)S(1)}, u32[]{:S(2)}, u32[]{:S(2)}) collective-permute-start(f32[39,96,3]{1,0,2:T(8,128)S(1)} %copy.21), channel_id=1, source_target_pairs={{16,0},{32,16},{48,32},{64,48},{80,64},{96,80},{112,96},{128,112},... | collective-permute-start | bytes 134792 | tf_op jit(solution)/shard_map/ppermute | solution.py:29
  40.2 2.1 %copy.20 = f32[39,96,3]{1,0,2:T(8,128)S(1)} copy(f32[39,96,3]{2,1,0:T(8,128)} %get-tuple-element.34) | data formatting | bytes 89856 | tf_op jit(solution)/shard_map/slice | solution.py:26
  42.3 1.9 %collective-permute-start = (f32[39,96,3]{1,0,2:T(8,128)S(1)}, f32[39,96,3]{1,0,2:T(8,128)S(1)}, u32[]{:S(2)}, u32[]{:S(2)}) collective-permute-start(f32[39,96,3]{1,0,2:T(8,128)S(1)} %copy.20), channel_id=1, source_target_pairs={{0,16},{16,32},{32,48},{48,64},{64,80},{80,96},{96,112},{112,128},... | collective-permute-start | bytes 134792 | tf_op jit(solution)/shard_map/ppermute | solution.py:28
  47.0 4.0 %collective-permute-done = f32[39,96,3]{1,0,2:T(8,128)S(1)} collective-permute-done((f32[39,96,3]{1,0,2:T(8,128)S(1)}, f32[39,96,3]{1,0,2:T(8,128)S(1)}, u32[]{:S(2)}, u32[]{:S(2)}) %collective-permute-start) | collective-permute-done | bytes 44960 | tf_op jit(solution)/shard_map/ppermute | solution.py:28
  51.0 1.9 %copy.22 = f32[39,96,3]{2,1,0:T(8,128)} copy(f32[39,96,3]{1,0,2:T(8,128)S(1)} %collective-permute-done) | data formatting | bytes 89856 | tf_op jit(solution)/shard_map/ppermute | solution.py:28
  52.9 1.9 %copy.23 = f32[39,96,3]{2,1,0:T(8,128)} copy(f32[39,96,3]{1,0,2:T(8,128)S(1)} %collective-permute-done.1) | data formatting | bytes 89856 | tf_op jit(solution)/shard_map/ppermute | solution.py:29
  54.8 2.2 %pad_maximum_fusion.5 = (f32[39,3,134]{2,1,0:T(4,128)}, f32[39,3,134]{2,1,0:T(4,128)}) fusion(f32[39,96,3]{2,1,0:T(8,128)} %copy.23, f32[39,96,128]{2,1,0:T(8,128)S(1)} %bitcast_dynamic-update-slice_fusion, f32[39,96,3]{2,1,0:T(8,128)} %copy.22), kind=kLoop, calls=%fused_computation.108 | loop fusion | flops 62712 | bytes 2132208 | tf_op jit(solution)/shard_map/slice | solution.py:37
  57.0 5.0 %collective-permute-start.2 = (f32[39,3,134]{2,1,0:T(4,128)}, f32[39,3,134]{2,1,0:T(4,128)S(1)}, u32[]{:S(2)}, u32[]{:S(2)}) collective-permute-start(f32[39,3,134]{2,1,0:T(4,128)} %get-tuple-element.22), channel_id=1, source_target_pairs={{0,1},{1,2},{2,3},{3,4},{4,5},{5,6},{6,7},{7,8},{8,9},{9,10},{10,1... | collective-permute-start | bytes 188144 | tf_op jit(solution)/shard_map/ppermute | solution.py:39
  62.0 1.9 %collective-permute-start.3 = (f32[39,3,134]{2,1,0:T(4,128)}, f32[39,3,134]{2,1,0:T(4,128)}, u32[]{:S(2)}, u32[]{:S(2)}) collective-permute-start(f32[39,3,134]{2,1,0:T(4,128)} %get-tuple-element.23), channel_id=1, source_target_pairs={{1,0},{2,1},{3,2},{4,3},{5,4},{6,5},{7,6},{8,7},{9,8},{10,9},{11,1... | collective-permute-start | bytes 188144 | tf_op jit(solution)/shard_map/ppermute | solution.py:40
  65.3 2.4 %collective-permute-done.2 = f32[39,3,134]{2,1,0:T(4,128)S(1)} collective-permute-done((f32[39,3,134]{2,1,0:T(4,128)}, f32[39,3,134]{2,1,0:T(4,128)S(1)}, u32[]{:S(2)}, u32[]{:S(2)}) %collective-permute-start.2) | collective-permute-done | bytes 62744 | tf_op jit(solution)/shard_map/ppermute | solution.py:39
  67.7 4.9 %collective-permute-done.3 = f32[39,3,134]{2,1,0:T(4,128)} collective-permute-done((f32[39,3,134]{2,1,0:T(4,128)}, f32[39,3,134]{2,1,0:T(4,128)}, u32[]{:S(2)}, u32[]{:S(2)}) %collective-permute-start.3) | collective-permute-done | bytes 62744 | tf_op jit(solution)/shard_map/ppermute | solution.py:40
  72.6 1.3 maximum_bitcast_fusion.2
  75.4 2.6 %pad_maximum_fusion = f32[39,102,134]{2,1,0:T(8,128)S(1)} fusion(f32[39,3,134]{2,1,0:T(4,128)} %collective-permute-done.3, f32[39,96,3]{2,1,0:T(8,128)S(1)} %copy-done.2, f32[39,96,128]{2,1,0:T(8,128)S(1)} %bitcast_dynamic-update-slice_fusion, f32[39,96,3]{2,1,0:T(8,128)S(1)} %copy-done.1, f32[39,3,134]{2,1,0:T(4,128)S(1)} %collective-permute-done.2), kind=kLoop, calls=%fused_computation | loop fusion | flops 2132208 | bytes 4264416 | tf_op jit(solution)/shard_map/concatenate | solution.py:41
  78.9 1.2 slice_add_fusion.3
  80.9 2.1 %slice_add_fusion = f32[24,100,132]{2,1,0:T(8,128)S(1)} fusion(f32[39,102,134]{2,1,0:T(8,128)S(1)} %pad_maximum_fusion), kind=kLoop, calls=%fused_computation.14 | loop fusion | flops 950400 | bytes 6336000 | tf_op jit(solution)/shard_map/add | solution.py:78
  83.0 7.1 %all-gather.2.cloned.1.call-done = f32[12,1664,128]{2,1,0:T(8,128)} async-done(((f32[12,104,128]{2,1,0:T(8,128)}), f32[12,1664,128]{2,1,0:T(8,128)}) %all-gather.2.cloned.1.call-update) | async-done | bytes 10223632 | tf_op jit(solution)/shard_map/all_gather | solution.py:118
  90.2 1.3 slice.278
  91.4 1.3 convolution_bitcast_fusion.1
  92.7 4.0 %collective-permute-start.6 = (f32[12,102,3]{1,0,2:T(8,128)S(1)}, f32[12,102,3]{1,0,2:T(8,128)S(1)}, u32[]{:S(2)}, u32[]{:S(2)}) collective-permute-start(f32[12,102,3]{1,0,2:T(8,128)S(1)} %get-tuple-element.61), channel_id=1, source_target_pairs={{0,16},{16,32},{32,48},{48,64},{64,80},{80,96},{96,112},{112,128},... | collective-permute-start | bytes 44072 | tf_op jit(solution)/shard_map/ppermute | solution.py:133
  96.7 6.9 %collective-permute-start.7 = (f32[12,102,3]{1,0,2:T(8,128)S(1)}, f32[12,102,3]{1,0,2:T(8,128)S(1)}, u32[]{:S(2)}, u32[]{:S(2)}) collective-permute-start(f32[12,102,3]{1,0,2:T(8,128)S(1)} %get-tuple-element.62), channel_id=1, source_target_pairs={{16,0},{32,16},{48,32},{64,48},{80,64},{96,80},{112,96},{128,112},... | collective-permute-start | bytes 44072 | tf_op jit(solution)/shard_map/ppermute | solution.py:134
  103.6 9.3 %convolution_bitcast_fusion = f32[12,102,128]{2,1,0:T(8,128)S(1)} fusion(f32[12,1664,128]{2,1,0:T(8,128)} %all-gather.2.cloned.1.call-done, f32[102,1664,1]{0,1,2:T(8,128)S(1)} %bitcast.40), kind=kOutput, calls=%fused_computation.46 | convolution fusion | flops 3128426496 | bytes 11529216 | tf_op jit(solution)/shard_map/rs,ksc->krc/dot_general | solution.py:136
  115.3 2.3 %slice_subtract_fusion.2 = f32[12,102,134]{2,1,0:T(8,128)S(1)} fusion(f32[39,102,134]{2,1,0:T(8,128)} %copy-done, f32[12,102,3]{2,1,0:T(8,128)} %copy.28, f32[12,102,128]{2,1,0:T(8,128)S(1)} %convolution_bitcast_fusion, f32[12,102,3]{2,1,0:T(8,128)} %copy.27), kind=kLoop, calls=%fused_computation.41 | loop fusion | flops 492048 | bytes 1968192 | tf_op jit(solution)/shard_map/sub | solution.py:138
  120.7 2.1 %fusion.2 = f32[24,98,130]{2,1,0:T(8,128)S(1)} fusion(f32[12,100,132]{2,1,0:T(8,128)S(1)} %get-tuple-element.53, f32[12,100,132]{2,1,0:T(8,128)S(1)} %get-tuple-element.52), kind=kLoop, calls=%fused_computation.9 | loop fusion | flops 2140320 | bytes 2490240 | tf_op jit(solution)/shard_map/add | solution.py:78
  126.1 1.8 %fusion.58 = (f32[12,96,128]{2,1,0:T(8,128)}, f32[12,96,128]{2,1,0:T(8,128)S(1)}, f32[12,96,128]{2,1,0:T(8,128)}) fusion(f32[12,98,130]{2,1,0:T(8,128)S(1)} %get-tuple-element.48, f32[96]{0:T(128)S(1)} %copy-done.30, f32[12,98,130]{2,1,0:T(8,128)S(1)} %get-tuple-element.47), kind=kLoop, calls=%fused_computation.141 | loop fusion | flops 737280 | bytes 5308800 | tf_op jit(solution)/shard_map/slice | solution.py:166
  (105 shorter events, 19.4 us)
Async XLA Ops:
  7.2 3.4 %copy-start.3 = (f32[12,96,128]{2,1,0:T(8,128)S(1)}, f32[12,96,128]{2,1,0:T(8,128)}, u32[]{:S(2)}) copy-start(f32[12,96,128]{2,1,0:T(8,128)} %param.12) | copy-start | bytes 1769476
  7.2 83.0 %all-gather.2.cloned.1.call-start = ((), (), s32[]{:S(2)}) async-start(), calls=%async_computation | async-start | bytes 10862592 | tf_op jit(solution)/shard_map/all_gather | solution.py:118
  8.8 1.7 %copy-start.7 = (f32[96,128]{1,0:T(8,128)}, f32[96,128]{1,0:T(8,128)S(1)}, u32[]{:S(2)}) copy-start(f32[96,128]{1,0:T(8,128)S(1)} %convert_element_type.10) | copy-start | bytes 147460
  10.5 2.1 %copy-start.9 = (f32[96,1536]{1,0:T(8,128)S(1)}, f32[96,1536]{1,0:T(8,128)}, u32[]{:S(2)}) copy-start(f32[96,1536]{1,0:T(8,128)} %param.20) | copy-start | bytes 1769476
  12.7 51.2 %collective-permute-start.4 = (f32[3,1536]{1,0:T(4,128)S(1)}, f32[3,1536]{1,0:T(4,128)S(1)}, u32[]{:S(2)}, u32[]{:S(2)}) collective-permute-start(f32[3,1536]{1,0:T(4,128)S(1)} %get-tuple-element.41), channel_id=1, source_target_pairs={{0,1},{1,2},{2,3},{3,4},{4,5},{5,6},{6,7},{7,8},{8,9},{9,10},{10,1... | collective-permute-start | bytes 55304 | tf_op jit(solution)/shard_map/ppermute | solution.py:39
  17.3 7.9 %copy-start.10 = (f32[12,96,128]{2,1,0:T(8,128)S(1)}, f32[12,96,128]{2,1,0:T(8,128)}, u32[]{:S(2)}) copy-start(f32[12,96,128]{2,1,0:T(8,128)} %param.15) | copy-start | bytes 1769476
  17.3 46.6 %collective-permute-start.5 = (f32[3,1536]{1,0:T(4,128)S(1)}, f32[3,1536]{1,0:T(4,128)S(1)}, u32[]{:S(2)}, u32[]{:S(2)}) collective-permute-start(f32[3,1536]{1,0:T(4,128)S(1)} %get-tuple-element.42), channel_id=1, source_target_pairs={{1,0},{2,1},{3,2},{4,3},{5,4},{6,5},{7,6},{8,7},{9,8},{10,9},{11,1... | collective-permute-start | bytes 55304 | tf_op jit(solution)/shard_map/ppermute | solution.py:40
  24.0 1.2 copy-start.19
  24.1 1.3 copy-start.20
  24.1 1.3 copy-start.18
  30.1 22.7 %collective-permute-start.1 = (f32[39,96,3]{1,0,2:T(8,128)S(1)}, f32[39,96,3]{1,0,2:T(8,128)S(1)}, u32[]{:S(2)}, u32[]{:S(2)}) collective-permute-start(f32[39,96,3]{1,0,2:T(8,128)S(1)} %copy.21), channel_id=1, source_target_pairs={{16,0},{32,16},{48,32},{64,48},{80,64},{96,80},{112,96},{128,112},... | collective-permute-start | bytes 134792 | tf_op jit(solution)/shard_map/ppermute | solution.py:29
  42.3 8.7 %collective-permute-start = (f32[39,96,3]{1,0,2:T(8,128)S(1)}, f32[39,96,3]{1,0,2:T(8,128)S(1)}, u32[]{:S(2)}, u32[]{:S(2)}) collective-permute-start(f32[39,96,3]{1,0,2:T(8,128)S(1)} %copy.20), channel_id=1, source_target_pairs={{0,16},{16,32},{32,48},{48,64},{64,80},{80,96},{96,112},{112,128},... | collective-permute-start | bytes 134792 | tf_op jit(solution)/shard_map/ppermute | solution.py:28
  57.0 10.7 %collective-permute-start.2 = (f32[39,3,134]{2,1,0:T(4,128)}, f32[39,3,134]{2,1,0:T(4,128)S(1)}, u32[]{:S(2)}, u32[]{:S(2)}) collective-permute-start(f32[39,3,134]{2,1,0:T(4,128)} %get-tuple-element.22), channel_id=1, source_target_pairs={{0,1},{1,2},{2,3},{3,4},{4,5},{5,6},{6,7},{7,8},{8,9},{9,10},{10,1... | collective-permute-start | bytes 188144 | tf_op jit(solution)/shard_map/ppermute | solution.py:39
  62.0 10.6 %collective-permute-start.3 = (f32[39,3,134]{2,1,0:T(4,128)}, f32[39,3,134]{2,1,0:T(4,128)}, u32[]{:S(2)}, u32[]{:S(2)}) collective-permute-start(f32[39,3,134]{2,1,0:T(4,128)} %get-tuple-element.23), channel_id=1, source_target_pairs={{1,0},{2,1},{3,2},{4,3},{5,4},{6,5},{7,6},{8,7},{9,8},{10,9},{11,1... | collective-permute-start | bytes 188144 | tf_op jit(solution)/shard_map/ppermute | solution.py:40
  72.6 2.8 %copy-start.1 = (f32[39,96,3]{2,1,0:T(8,128)S(1)}, f32[39,96,3]{2,1,0:T(8,128)}, u32[]{:S(2)}) copy-start(f32[39,96,3]{2,1,0:T(8,128)} %copy.22) | copy-start | bytes 134788
  72.6 2.8 %copy-start.2 = (f32[39,96,3]{2,1,0:T(8,128)S(1)}, f32[39,96,3]{2,1,0:T(8,128)}, u32[]{:S(2)}) copy-start(f32[39,96,3]{2,1,0:T(8,128)} %copy.23) | copy-start | bytes 134788
  78.0 2.9 %copy-start = (f32[39,102,134]{2,1,0:T(8,128)}, f32[39,102,134]{2,1,0:T(8,128)S(1)}, u32[]{:S(2)}) copy-start(f32[39,102,134]{2,1,0:T(8,128)S(1)} %pad_maximum_fusion) | copy-start | bytes 6396628
  90.2 13.4 %copy-start.4 = (f32[102,16,104]{0,2,1:T(8,128)S(1)}, f32[102,16,104]{0,2,1:T(8,128)}, u32[]{:S(2)}) copy-start(f32[102,16,104]{0,2,1:T(8,128)} %pad.9) | copy-start | bytes 2036740
  92.7 21.4 %collective-permute-start.6 = (f32[12,102,3]{1,0,2:T(8,128)S(1)}, f32[12,102,3]{1,0,2:T(8,128)S(1)}, u32[]{:S(2)}, u32[]{:S(2)}) collective-permute-start(f32[12,102,3]{1,0,2:T(8,128)S(1)} %get-tuple-element.61), channel_id=1, source_target_pairs={{0,16},{16,32},{32,48},{48,64},{64,80},{80,96},{96,112},{112,128},... | collective-permute-start | bytes 44072 | tf_op jit(solution)/shard_map/ppermute | solution.py:133
  96.7 16.3 %collective-permute-start.7 = (f32[12,102,3]{1,0,2:T(8,128)S(1)}, f32[12,102,3]{1,0,2:T(8,128)S(1)}, u32[]{:S(2)}, u32[]{:S(2)}) collective-permute-start(f32[12,102,3]{1,0,2:T(8,128)S(1)} %get-tuple-element.62), channel_id=1, source_target_pairs={{16,0},{32,16},{48,32},{64,48},{80,64},{96,80},{112,96},{128,112},... | collective-permute-start | bytes 44072 | tf_op jit(solution)/shard_map/ppermute | solution.py:134
  115.2 2.3 %copy-start.12 = (f32[100,132]{1,0:T(8,128)S(1)}, f32[100,132]{1,0:T(8,128)}, u32[]{:S(2)}) copy-start(f32[100,132]{1,0:T(8,128)} %get-tuple-element.57) | copy-start | bytes 158404
  115.2 2.3 %copy-start.13 = (f32[100,132]{1,0:T(8,128)S(1)}, f32[100,132]{1,0:T(8,128)}, u32[]{:S(2)}) copy-start(f32[100,132]{1,0:T(8,128)} %get-tuple-element.58) | copy-start | bytes 158404
  115.2 2.3 %copy-start.31 = (f32[100]{0:T(128)S(1)}, f32[100]{0:T(128)}, u32[]{:S(2)}) copy-start(f32[100]{0:T(128)} %slice_multiply_fusion.8) | copy-start | bytes 1204
  117.5 1.2 copy-start.5
  117.6 1.2 copy-start.6
  117.6 1.2 copy-start.17
  117.6 1.2 copy-start.21
  117.6 1.2 copy-start.22
  117.6 1.2 copy-start.24
  120.7 2.1 %copy-start.11 = (f32[98,130]{1,0:T(8,128)S(1)}, f32[98,130]{1,0:T(8,128)}, u32[]{:S(2)}) copy-start(f32[98,130]{1,0:T(8,128)} %get-tuple-element.69) | copy-start | bytes 152884
  126.1 1.9 %copy-start.29 = (f32[6]{0:T(128)S(1)}, f32[6]{0:T(128)}, u32[]{:S(2)}) copy-start(f32[6]{0:T(128)} %constant.48) | copy-start | bytes 76
  126.1 2.0 %copy-start.8 = (f32[96,128]{1,0:T(8,128)S(1)}, f32[96,128]{1,0:T(8,128)}, u32[]{:S(2)}) copy-start(f32[96,128]{1,0:T(8,128)} %copy-done.7) | copy-start | bytes 147460
  (9 other events, 8.4 us)
Sparse Core Ops, SparseCore 0:
  12.8 77.3 all-gather.1
where the time goes:
time: 137 us; the launch traced here: 136 us
  starting transfers between devices  40 us (29%)
  other arithmetic  28.6 us (21%)
  local copies, waits for them, and re-layouts  20.5 us (15%)
  waiting for transfers between devices  18.5 us (14%)
  between operations  14.7 us (11%)
  matrix products  13.5 us (10%)
    ppermute x1, starting transfers between devices, widen_lon(): after = lax.ppermute(initial, 'lon', down)  10 us
    ppermute x2, starting transfers between devices, widen_lat(): before = lax.ppermute(last, LAT, up)  9.59 us
    dot_general x1, matrix products, per_device(): jnp.einsum('rs,ksc->krc', green_pad, gathered, precision=lax.Precision.HI...  9.34 us
    ppermute x2, starting transfers between devices, widen_lat(): after = lax.ppermute(initial, LAT, down)  7.52 us
    all_gather x1, waiting for transfers between devices, per_device(): gathered = lax.all_gather(packed, LAT, axis=1, tiled=True)  7.14 us
    ppermute x1, starting transfers between devices, per_device(): after = lax.ppermute(edge_sal[:, :, :HALO], 'lon', down)  6.9 us
    ppermute x2, waiting for transfers between devices, widen_lat(): after = lax.ppermute(initial, LAT, down)  4.93 us
    slice x2, local copies, waits for them, and re-layouts, widen_lon(): last = lax.slice_in_dim(array, length - width, length, axis=dim)  4.77 us
  transfers between devices with their start and end apart: 9, of which 4 were waited for; matrix products, arithmetic and copies ran while one was open for 30% of the time, Pallas kernels for 0%

commit v1 on v0

--- a/solution.py
+++ b/solution.py
@@ -9,6 +9,13 @@
 VISCOSITY = 0.5
 HALO = 3
 LAT = ("chip", "core")
+
+
+def swapped_in(x, axis, d):
+    size = lax.axis_size(axis)
+    shards = jnp.stack([x for _ in range(size)])
+    shards = lax.all_to_all(shards, axis, split_axis=0, concat_axis=0)
+    return jnp.concatenate(shards, axis=d)
 
 
 def lat_index():
@@ -115,7 +122,7 @@
     spare = 8 * ((2 * HALO + 7) // 8)
     edges = jnp.pad(edges, ((0, 0), (0, spare - 2 * HALO), (0, columns - rows_here)))
     packed = jnp.concatenate([mixed, edges], axis=1)
-    gathered = lax.all_gather(packed, LAT, axis=1, tiled=True)
+    gathered = swapped_in(packed, LAT, 1)
     fields = jnp.stack([ocean_depth, bottom_drag, wet_frac], axis=0)
     stack = jnp.concatenate([elevation - equilibrium, transport_u, transport_v, fields], axis=0)
     stack = widen_lat(widen_lon(stack, HALO, 2), HALO, 1)

time: 137 us -> 258 us (1.88)
  waiting for transfers between devices: 18.5 us -> 128 us
  local copies, waits for them, and re-layouts: 20.5 us -> 35.5 us
  between operations: 14.7 us -> 1.26 us
  starting transfers between devices: 40 us -> 49.2 us
    ppermute x1, waiting for transfers between devices: 0.01 us -> 126 us  [widen_lon(): after = lax.ppermute(initial, 'lon', down)]
    all_to_all x0 -> x1, starting transfers between devices: none -> 11.6 us  [swapped_in(): shards = lax.all_to_all(shards, axis, split_axis=0, concat_axis=0)]
    all_to_all x0 -> x1, local copies, waits for them, and re-layouts: none -> 11 us  [swapped_in(): shards = lax.all_to_all(shards, axis, split_axis=0, concat_axis=0)]
    all_gather x1 -> x0, waiting for transfers between devices: 7.14 us -> none  [per_device(): gathered = lax.all_gather(packed, LAT, axis=1, tiled=True)]
    another operation x0 -> x1, local copies, waits for them, and re-layouts: none -> 4.92 us  [swapped_in(): shards = jnp.stack([x for _ in range(size)])]
    ppermute x2, waiting for transfers between devices: 4.93 us -> 0.65 us  [widen_lat(): after = lax.ppermute(initial, LAT, down)]
    ppermute x1, waiting for transfers between devices: 4 us -> 0.01 us  [widen_lon(): before = lax.ppermute(last, 'lon', up)]
    ppermute x1, starting transfers between devices: 6.9 us -> 10.1 us  [per_device(): after = lax.ppermute(edge_sal[:, :, :HALO], 'lon', down)]
  transfers between devices with their start and end apart: 9 -> 9, of which waited for: 4 -> 3; matrix products, arithmetic and copies ran while one was open for 30% -> 15% of each run, Pallas kernels for 0% -> 0%
where the time goes in v1:
time: 258 us; the launch traced here: 257 us
  waiting for transfers between devices  128 us (50%)
  starting transfers between devices  49.2 us (19%)
  local copies, waits for them, and re-layouts  35.5 us (14%)
  other arithmetic  26.4 us (10%)
  matrix products  16 us (6%)
    ppermute x1, waiting for transfers between devices, widen_lon(): after = lax.ppermute(initial, 'lon', down)  126 us
    all_to_all x1, starting transfers between devices, swapped_in(): shards = lax.all_to_all(shards, axis, split_axis=0, concat_axis=0)  11.6 us
    all_to_all x1, local copies, waits for them, and re-layouts, swapped_in(): shards = lax.all_to_all(shards, axis, split_axis=0, concat_axis=0)  11 us
    ppermute x1, starting transfers between devices, per_device(): after = lax.ppermute(edge_sal[:, :, :HALO], 'lon', down)  10.1 us
    ppermute x2, starting transfers between devices, widen_lat(): before = lax.ppermute(last, LAT, up)  10.1 us
    dot_general x1, matrix products, per_device(): jnp.einsum('rs,ksc->krc', green_pad, gathered, precision=lax.Precision.HI...  9.86 us
    ppermute x1, starting transfers between devices, widen_lon(): after = lax.ppermute(initial, 'lon', down)  8.75 us
  transfers between devices with their start and end apart: 9, of which 3 were waited for; matrix products, arithmetic and copies ran while one was open for 15% of the time, Pallas kernels for 0%

profile of v1, /device:TPU:1, one launch (start us, length us, event | category | flops | bytes accessed | tf_op | source)
XLA Modules:
  0.0 256.7 jit_solution(11137430548888813602)
XLA Ops:
  2.2 1.7 fusion.52
  3.9 2.2 convolution_bitcast_fusion.1
  6.2 4.9 %stack.8 = f32[16,12,104,128]{3,2,1,0:T(8,128)} broadcast(f32[12,104,128]{2,1,0:T(8,128)S(1)} %select_maximum_fusion), dimensions={1,2,3} | broadcast | bytes 10862592 | tf_op jit(solution)/shard_map/stack | solution.py:16
  11.1 11.6 %all-to-all-start = ((f32[16,12,104,128]{3,2,1,0:T(8,128)}), f32[16,12,104,128]{3,2,1,0:T(8,128)}, u32[]{:S(2)}, u32[]{:S(2)}) async-start(f32[16,12,104,128]{3,2,1,0:T(8,128)} %stack.8), calls=%async_computation | async-start | bytes 20447232 | tf_op jit(solution)/shard_map/all_to_all | solution.py:17
  24.1 2.6 %fusion.65 = (f32[39,96,3]{2,1,0:T(8,128)}, f32[39,96,3]{2,1,0:T(8,128)}) fusion(f32[39,96,128]{2,1,0:T(8,128)S(1)} %bitcast_dynamic-update-slice_fusion), kind=kLoop, calls=%fused_computation.146 | loop fusion | bytes 179712 | tf_op jit(solution)/shard_map/slice | solution.py:33
  26.7 2.2 copy.22
  28.9 8.8 %collective-permute-start.1 = (f32[39,96,3]{1,0,2:T(8,128)S(1)}, f32[39,96,3]{1,0,2:T(8,128)S(1)}, u32[]{:S(2)}, u32[]{:S(2)}) collective-permute-start(f32[39,96,3]{1,0,2:T(8,128)S(1)} %copy.22), channel_id=1, source_target_pairs={{16,0},{32,16},{48,32},{64,48},{80,64},{96,80},{112,96},{128,112},... | collective-permute-start | bytes 134792 | tf_op jit(solution)/shard_map/ppermute | solution.py:36
  37.6 2.1 copy.21
  39.7 1.9 collective-permute-start
  41.7 2.4 collective-permute-start.5
  44.1 3.4 %collective-permute-start.4 = (f32[3,1536]{1,0:T(4,128)S(1)}, f32[3,1536]{1,0:T(4,128)S(1)}, u32[]{:S(2)}, u32[]{:S(2)}) collective-permute-start(f32[3,1536]{1,0:T(4,128)S(1)} %get-tuple-element.41), channel_id=1, source_target_pairs={{0,1},{1,2},{2,3},{3,4},{4,5},{5,6},{6,7},{7,8},{8,9},{9,10},{10,1... | collective-permute-start | bytes 55304 | tf_op jit(solution)/shard_map/ppermute | solution.py:46
  50.1 126.3 %collective-permute-done.1 = f32[39,96,3]{1,0,2:T(8,128)S(1)} collective-permute-done((f32[39,96,3]{1,0,2:T(8,128)S(1)}, f32[39,96,3]{1,0,2:T(8,128)S(1)}, u32[]{:S(2)}, u32[]{:S(2)}) %collective-permute-start.1) | collective-permute-done | bytes 44960 | tf_op jit(solution)/shard_map/ppermute | solution.py:36
  176.4 1.9 copy.24
  178.4 2.0 copy.23
  180.4 2.2 pad_maximum_fusion.5
  182.5 2.5 collective-permute-start.3
  185.0 6.7 %collective-permute-start.2 = (f32[39,3,134]{2,1,0:T(4,128)}, f32[39,3,134]{2,1,0:T(4,128)}, u32[]{:S(2)}, u32[]{:S(2)}) collective-permute-start(f32[39,3,134]{2,1,0:T(4,128)} %get-tuple-element.22), channel_id=1, source_target_pairs={{0,1},{1,2},{2,3},{3,4},{4,5},{5,6},{6,7},{7,8},{8,9},{9,10},{10,1... | collective-permute-start | bytes 188144 | tf_op jit(solution)/shard_map/ppermute | solution.py:46
  192.8 1.3 collective-permute-done.2
  194.1 1.1 maximum_bitcast_fusion.2
  196.7 2.6 %pad_maximum_fusion = f32[39,102,134]{2,1,0:T(8,128)S(1)} fusion(f32[39,3,134]{2,1,0:T(4,128)S(1)} %collective-permute-done.3, f32[39,96,3]{2,1,0:T(8,128)S(1)} %copy-done.1, f32[39,96,128]{2,1,0:T(8,128)S(1)} %bitcast_dynamic-update-slice_fusion, f32[39,96,3]{2,1,0:T(8,128)S(1)} %copy-done.2, f32[39,3,134]{2,1,0:T(4,128)} %collective-permute-done.2), kind=kLoop, calls=%fused_computation.3 | loop fusion | flops 2132208 | bytes 4264416 | tf_op jit(solution)/shard_map/concatenate | solution.py:48
  200.2 1.2 slice_add_fusion.3
  202.3 2.1 slice_add_fusion
  204.4 11.0 %copy.37 = f32[16,12,104,128]{3,1,0,2:T(8,128)} copy(f32[16,12,104,128]{3,2,1,0:T(8,128)} %all-to-all-done) | data formatting | bytes 20447232 | tf_op jit(solution)/shard_map/all_to_all | solution.py:17
  215.4 2.2 convolution_bitcast_fusion
  218.2 10.1 %collective-permute-start.7 = (f32[12,102,3]{1,0,2:T(8,128)S(1)}, f32[12,102,3]{1,0,2:T(8,128)}, u32[]{:S(2)}, u32[]{:S(2)}) collective-permute-start(f32[12,102,3]{1,0,2:T(8,128)S(1)} %get-tuple-element.62), channel_id=1, source_target_pairs={{16,0},{32,16},{48,32},{64,48},{80,64},{96,80},{112,96},{128,112},... | collective-permute-start | bytes 44072 | tf_op jit(solution)/shard_map/ppermute | solution.py:141
  228.3 1.9 collective-permute-start.6
  230.2 9.9 %fusion.14 = f32[12,102,128]{2,1,0:T(8,128)} fusion(f32[16,12,104,128]{3,2,1,0:T(8,128)} %all-to-all-done, f32[102,16,96]{0,2,1:T(8,128)S(1)} %bitcast.51), kind=kOutput, calls=%fused_computation.49 | convolution fusion | flops 3128426496 | bytes 11476992 | tf_op jit(solution)/shard_map/rs,ksc->krc/dot_general | solution.py:143
  241.1 1.9 copy.29
  243.0 2.3 slice_subtract_fusion.2
  245.4 1.1 fusion.12
  248.5 2.1 fusion.4
  253.8 1.8 fusion.66
  (106 shorter events, 17.5 us)
Async XLA Ops:
  1.4 2.4 copy-start.6
  11.1 11.6 %copy-start.3 = (f32[12,96,128]{2,1,0:T(8,128)S(1)}, f32[12,96,128]{2,1,0:T(8,128)}, u32[]{:S(2)}) copy-start(f32[12,96,128]{2,1,0:T(8,128)} %param.12) | copy-start | bytes 1769476
  11.1 11.6 %copy-start.9 = (f32[12,96,128]{2,1,0:T(8,128)S(1)}, f32[12,96,128]{2,1,0:T(8,128)}, u32[]{:S(2)}) copy-start(f32[12,96,128]{2,1,0:T(8,128)} %param.13) | copy-start | bytes 1769476
  11.1 193.3 %all-to-all-start = ((f32[16,12,104,128]{3,2,1,0:T(8,128)}), f32[16,12,104,128]{3,2,1,0:T(8,128)}, u32[]{:S(2)}, u32[]{:S(2)}) async-start(f32[16,12,104,128]{3,2,1,0:T(8,128)} %stack.8), calls=%async_computation | async-start | bytes 20447232 | tf_op jit(solution)/shard_map/all_to_all | solution.py:17
  22.7 1.2 copy-start.11
  22.7 1.3 copy-start.20
  22.7 1.3 copy-start.21
  22.8 1.3 copy-start.19
  26.7 15.0 %copy-start.8 = (f32[96,1536]{1,0:T(8,128)S(1)}, f32[96,1536]{1,0:T(8,128)}, u32[]{:S(2)}) copy-start(f32[96,1536]{1,0:T(8,128)} %param.20) | copy-start | bytes 1769476
  28.9 147.6 %collective-permute-start.1 = (f32[39,96,3]{1,0,2:T(8,128)S(1)}, f32[39,96,3]{1,0,2:T(8,128)S(1)}, u32[]{:S(2)}, u32[]{:S(2)}) collective-permute-start(f32[39,96,3]{1,0,2:T(8,128)S(1)} %copy.22), channel_id=1, source_target_pairs={{16,0},{32,16},{48,32},{64,48},{80,64},{96,80},{112,96},{128,112},... | collective-permute-start | bytes 134792 | tf_op jit(solution)/shard_map/ppermute | solution.py:36
  39.7 138.6 %collective-permute-start = (f32[39,96,3]{1,0,2:T(8,128)S(1)}, f32[39,96,3]{1,0,2:T(8,128)S(1)}, u32[]{:S(2)}, u32[]{:S(2)}) collective-permute-start(f32[39,96,3]{1,0,2:T(8,128)S(1)} %copy.21), channel_id=1, source_target_pairs={{0,16},{16,32},{32,48},{48,64},{64,80},{80,96},{96,112},{112,128},... | collective-permute-start | bytes 134792 | tf_op jit(solution)/shard_map/ppermute | solution.py:35
  41.7 150.0 %collective-permute-start.5 = (f32[3,1536]{1,0:T(4,128)S(1)}, f32[3,1536]{1,0:T(4,128)S(1)}, u32[]{:S(2)}, u32[]{:S(2)}) collective-permute-start(f32[3,1536]{1,0:T(4,128)S(1)} %get-tuple-element.42), channel_id=1, source_target_pairs={{1,0},{2,1},{3,2},{4,3},{5,4},{6,5},{7,6},{8,7},{9,8},{10,9},{11,1... | collective-permute-start | bytes 55304 | tf_op jit(solution)/shard_map/ppermute | solution.py:47
  44.1 147.7 %collective-permute-start.4 = (f32[3,1536]{1,0:T(4,128)S(1)}, f32[3,1536]{1,0:T(4,128)S(1)}, u32[]{:S(2)}, u32[]{:S(2)}) collective-permute-start(f32[3,1536]{1,0:T(4,128)S(1)} %get-tuple-element.41), channel_id=1, source_target_pairs={{0,1},{1,2},{2,3},{3,4},{4,5},{5,6},{6,7},{7,8},{8,9},{9,10},{10,1... | collective-permute-start | bytes 55304 | tf_op jit(solution)/shard_map/ppermute | solution.py:46
  182.5 10.2 %collective-permute-start.3 = (f32[39,3,134]{2,1,0:T(4,128)}, f32[39,3,134]{2,1,0:T(4,128)S(1)}, u32[]{:S(2)}, u32[]{:S(2)}) collective-permute-start(f32[39,3,134]{2,1,0:T(4,128)} %get-tuple-element.23), channel_id=1, source_target_pairs={{1,0},{2,1},{3,2},{4,3},{5,4},{6,5},{7,6},{8,7},{9,8},{10,9},{11,1... | collective-permute-start | bytes 188144 | tf_op jit(solution)/shard_map/ppermute | solution.py:47
  185.0 9.0 %collective-permute-start.2 = (f32[39,3,134]{2,1,0:T(4,128)}, f32[39,3,134]{2,1,0:T(4,128)}, u32[]{:S(2)}, u32[]{:S(2)}) collective-permute-start(f32[39,3,134]{2,1,0:T(4,128)} %get-tuple-element.22), channel_id=1, source_target_pairs={{0,1},{1,2},{2,3},{3,4},{4,5},{5,6},{6,7},{7,8},{8,9},{9,10},{10,1... | collective-permute-start | bytes 188144 | tf_op jit(solution)/shard_map/ppermute | solution.py:46
  192.1 4.6 %copy-start.1 = (f32[39,96,3]{2,1,0:T(8,128)S(1)}, f32[39,96,3]{2,1,0:T(8,128)}, u32[]{:S(2)}) copy-start(f32[39,96,3]{2,1,0:T(8,128)} %copy.24) | copy-start | bytes 134788
  192.1 4.6 %copy-start.2 = (f32[39,96,3]{2,1,0:T(8,128)S(1)}, f32[39,96,3]{2,1,0:T(8,128)}, u32[]{:S(2)}) copy-start(f32[39,96,3]{2,1,0:T(8,128)} %copy.23) | copy-start | bytes 134788
  199.3 2.9 %copy-start = (f32[39,102,134]{2,1,0:T(8,128)}, f32[39,102,134]{2,1,0:T(8,128)S(1)}, u32[]{:S(2)}) copy-start(f32[39,102,134]{2,1,0:T(8,128)S(1)} %pad_maximum_fusion) | copy-start | bytes 6396628
  218.2 21.9 %collective-permute-start.7 = (f32[12,102,3]{1,0,2:T(8,128)S(1)}, f32[12,102,3]{1,0,2:T(8,128)}, u32[]{:S(2)}, u32[]{:S(2)}) collective-permute-start(f32[12,102,3]{1,0,2:T(8,128)S(1)} %get-tuple-element.62), channel_id=1, source_target_pairs={{16,0},{32,16},{48,32},{64,48},{80,64},{96,80},{112,96},{128,112},... | collective-permute-start | bytes 44072 | tf_op jit(solution)/shard_map/ppermute | solution.py:141
  228.3 12.8 %collective-permute-start.6 = (f32[12,102,3]{1,0,2:T(8,128)}, f32[12,102,3]{1,0,2:T(8,128)}, u32[]{:S(2)}, u32[]{:S(2)}) collective-permute-start(f32[12,102,3]{1,0,2:T(8,128)} %get-tuple-element.61), channel_id=1, source_target_pairs={{0,16},{16,32},{32,48},{48,64},{64,80},{80,96},{96,112},{112,128},... | collective-permute-start | bytes 44072 | tf_op jit(solution)/shard_map/ppermute | solution.py:140
  243.0 2.3 copy-start.13
  243.0 2.3 copy-start.14
  243.0 2.3 copy-start.32
  245.3 1.2 copy-start.4
  245.3 1.2 copy-start.5
  245.3 1.2 copy-start.18
  245.3 1.2 copy-start.22
  245.3 1.2 copy-start.23
  245.3 1.2 copy-start.25
  248.5 2.1 copy-start.12
  253.8 1.9 copy-start.30
  253.8 2.0 copy-start.7
  (10 other events, 9.4 us)
